TPU v7x, 256 devices: a whole 4x4x8 slice. The times are simulated.
256 devices in a mesh: dp: 4 (over y), expert: 64 (over z, x, core).
Axes of the slice: x: 4, y: 4, z: 8, core: 2. Of those that a mesh axis runs over, the one named last changes fastest.
Arguments:
- tokens: bfloat16 [4096, 2048], P('expert'), may hold values from -6 to 6
- attn_gain: float32 [2048], replicated, may hold values from 0.5 to 1.5
- w_query: bfloat16 [2048, 2048], P('expert', 'dp'), may hold values from -0.125 to 0.125
- w_key: bfloat16 [2048, 2048], P('expert', 'dp'), may hold values from -0.125 to 0.125
- w_value: bfloat16 [2048, 2048], P('expert', 'dp'), may hold values from -0.125 to 0.125
- w_out: bfloat16 [2048, 2048], P('expert', 'dp'), may hold values from -0.125 to 0.125
- cache: bfloat16 [131072, 4096], P('expert', 'dp')
- page_table: int32 [64, 16], P('expert'), may hold values from 0 to 15, each once within a row
- cache_len: int32 [64, 4], P('expert'), may hold values from 1 to 512, 1024 in all within a row
- new_len: int32 [64, 4], P('expert'), may hold values from 1 to 32, 64 in all within a row
- kv_owner: int32 [4096, 1], P('expert'), may hold values from 0 to 63; in each aligned block of 64 rows (0 to 63, 64 to 127, ...) at most 2 rows name the same one
- moe_gain: float32 [2048], replicated, may hold values from 0.5 to 1.5
- w_gate: bfloat16 [64, 2048, 1024], P('expert', None, 'dp'), may hold values from -0.125 to 0.125
- w_up: bfloat16 [64, 2048, 1024], P('expert', None, 'dp'), may hold values from -0.125 to 0.125
- w_down: bfloat16 [64, 1024, 2048], P('expert', 'dp'), may hold values from -0.1875 to 0.1875
- expert_ids: int32 [4096, 8], P('expert'), may hold values from 0 to 63, all different within a row; in each aligned block of 64 rows (0 to 63, 64 to 127, ...) at most 16 rows name the same one
- gate_weights: float32 [4096, 8], P('expert'), may hold values from 0.05 to 0.5
Outputs:
- out: bfloat16 [4096, 2048], P('expert')
- new_rows: bfloat16 [8192, 4096], P('expert', 'dp')
Inputs may be any that keep to these rules, and one draw needn't show every extreme that they name: `page_table`: each row of one index of the expert axis lists every local page once; request r reserves the pages in entries r * 4 to (r+1) * 4 - 1. `cache_len`: the lengths of one index sum to 4 * 4 * 128 // 2, and one of them equals 512. `new_len`: the new tokens of one index sum to 64 and stand request by request; one request has exactly 64 // 2. `kv_owner`: among the rows of one device no owner is named more than 2 times; some owner is named exactly 2 times. `expert_ids`: each row names distinct experts; among the rows of one device no expert is named more than 16 times, a bound that some block reaches.
All inputs are finite; a program needn't handle non-finite values.
Results may differ from a plain program's by a relative error of at most 0.012.
The roundings to bfloat16 on the way count: a program that leaves them out, or rounds other values in their place, can miss the bound.
Values may be sent and summed in bfloat16 or wider, within the bound.
No kernel may reach another device: no remote copies, remote signals or barrier semaphores. Data moves between devices by JAX's collectives and lax.ppermute only.
A program may use at most 64 MiB of HBM per device.

v0:
```python
import jax
import jax.numpy as jnp
from jax import lax
from jax.sharding import PartitionSpec as P

HD = 128
PAGE = 128
EPSILON = 1e-05


def norm_rows(row_data, gain_vec):
    mean_sq = jnp.mean(row_data * row_data, axis=-1, keepdims=True)
    return (row_data * lax.rsqrt(mean_sq + EPSILON) * gain_vec).astype(jnp.bfloat16)


def route_rank(route_ids, block_rows, id_range):
    row_total = route_ids.shape[0]
    labels = jnp.arange(id_range, dtype=jnp.int32)
    counts = jnp.sum((route_ids[:, :, None] == labels[None, None, :]).astype(jnp.int32), axis=1)
    counts = counts.reshape(row_total // block_rows, block_rows, id_range)
    before = (jnp.cumsum(counts, axis=1) - counts).reshape(row_total, id_range)
    return jnp.take_along_axis(before, route_ids, axis=1)


def key_masks(table_row, cache_lens, new_lens, row_count, page_size):
    req_count = cache_lens.shape[0]
    pages_here = table_row.shape[0]
    per_request = pages_here // req_count
    slot_ids = jnp.arange(pages_here, dtype=jnp.int32)
    matches = (table_row[:, None] == slot_ids[None, :]).astype(jnp.int32)
    slot_of_page = jnp.sum(matches * slot_ids[:, None], axis=0)
    page_request = slot_of_page // per_request
    page_start = slot_of_page % per_request * page_size
    key_request = jnp.repeat(page_request, page_size)
    key_position = jnp.repeat(page_start, page_size) + jnp.tile(
        jnp.arange(page_size, dtype=jnp.int32), pages_here
    )
    request_ids = jnp.arange(req_count, dtype=jnp.int32)
    key_length = jnp.sum(
        (key_request[:, None] == request_ids[None, :]).astype(jnp.int32) * cache_lens[None, :],
        axis=1,
    )
    request_ends = jnp.cumsum(new_lens)
    tok_ids = jnp.arange(row_count, dtype=jnp.int32)
    tok_request = jnp.sum((tok_ids[:, None] >= request_ends[None, :]).astype(jnp.int32), axis=1)
    cached = (tok_request[:, None] == key_request[None, :]) & (key_position < key_length)[None, :]
    fresh_mask = tok_request[:, None] == tok_request[None, :]
    return jnp.concatenate([cached, fresh_mask], axis=1)


def expert_block(routed, w_gate, w_up, w_down):
    gate_proj = jnp.einsum("necd,edf->necf", routed, w_gate, preferred_element_type=jnp.float32)
    up_proj = jnp.einsum("necd,edf->necf", routed, w_up, preferred_element_type=jnp.float32)
    active = (jax.nn.silu(gate_proj) * up_proj).astype(jnp.bfloat16)
    return jnp.einsum("necf,efd->necd", active, w_down, preferred_element_type=jnp.float32).astype(
        jnp.bfloat16
    )


def local(
    tokens,
    attn_gain,
    w_query,
    w_key,
    w_value,
    w_out,
    cache,
    page_table,
    cache_len,
    new_len,
    kv_owner,
    moe_gain,
    w_gate,
    w_up,
    w_down,
    expert_ids,
    gate_weights,
):
    row_count, model_width = tokens.shape
    n_expert = lax.axis_size("expert")
    local_experts = w_gate.shape[0]
    experts_all = n_expert * local_experts
    top_count = expert_ids.shape[1]
    capacity = min(row_count, 2 * row_count * top_count // experts_all)
    kv_cap = max(2, 2 * row_count // n_expert)
    head_group = w_query.shape[1] // HD
    full_query, full_key, full_value, full_out = (
        lax.all_gather(w_query, "expert", axis=0, tiled=True),
        lax.all_gather(w_key, "expert", axis=0, tiled=True),
        lax.all_gather(w_value, "expert", axis=0, tiled=True),
        lax.all_gather(w_out, "expert", axis=0, tiled=True),
    )
    resid_in = tokens.astype(jnp.float32)
    normed = norm_rows(resid_in, attn_gain)
    queries = jnp.dot(normed, full_query, preferred_element_type=jnp.float32).astype(jnp.bfloat16)
    new_keys = jnp.dot(normed, full_key, preferred_element_type=jnp.float32).astype(jnp.bfloat16)
    new_values = jnp.dot(normed, full_value, preferred_element_type=jnp.float32).astype(
        jnp.bfloat16
    )
    cache_count = cache.shape[0]
    split_cache = cache.reshape(cache_count, 2, head_group, HD)
    all_keys = jnp.concatenate(
        [split_cache[:, 0], new_keys.reshape(row_count, head_group, HD)], axis=0
    )
    all_values = jnp.concatenate(
        [split_cache[:, 1], new_values.reshape(row_count, head_group, HD)], axis=0
    )
    scores = jnp.einsum(
        "thc,rhc->htr",
        queries.reshape(row_count, head_group, HD),
        all_keys,
        preferred_element_type=jnp.float32,
    ) * HD ** (-0.5)
    valid_mask = key_masks(page_table[0], cache_len[0], new_len[0], row_count, PAGE)
    scores = jnp.where(valid_mask[None, :, :], scores, -1e30)
    highest = jnp.max(scores, axis=-1, keepdims=True)
    weights = jnp.exp(scores - highest)
    probs = (weights / jnp.sum(weights, axis=-1, keepdims=True)).astype(jnp.bfloat16)
    heads_out = (
        jnp.einsum("htr,rhc->thc", probs, all_values, preferred_element_type=jnp.float32)
        .astype(jnp.bfloat16)
        .reshape(row_count, head_group * HD)
    )
    attn_part = jnp.einsum("tc,dc->td", heads_out, full_out, preferred_element_type=jnp.float32)
    attn_out = lax.psum(attn_part.astype(jnp.bfloat16), "dp").astype(jnp.float32)
    residual = resid_in + attn_out
    moe_in = norm_rows(residual, moe_gain)
    kv_row = jnp.concatenate([new_keys, new_values], axis=1)
    kv_rank = route_rank(kv_owner, row_count, n_expert)[:, 0]
    kv_buffer = (
        jnp.zeros((n_expert, kv_cap, kv_row.shape[1]), jnp.bfloat16)
        .at[kv_owner[:, 0], kv_rank]
        .set(kv_row)
    )
    slot_rank = route_rank(expert_ids, row_count, experts_all)
    spread_rows = jnp.broadcast_to(moe_in[:, None, :], (row_count, top_count, model_width))
    tok_buffer = (
        jnp.zeros((experts_all, capacity, model_width), jnp.bfloat16)
        .at[expert_ids, slot_rank]
        .set(spread_rows)
    )
    tok_buffer = tok_buffer.reshape(n_expert, local_experts, capacity, model_width)
    got_rows, got_kv = (
        lax.all_to_all(tok_buffer, "expert", split_axis=0, concat_axis=0, tiled=True),
        lax.all_to_all(kv_buffer, "expert", split_axis=0, concat_axis=0, tiled=True),
    )
    partial_value = expert_block(got_rows, w_gate, w_up, w_down)
    returned = lax.all_to_all(
        partial_value, "expert", split_axis=0, concat_axis=0, tiled=True
    ).reshape(experts_all, capacity, model_width)
    picked = returned[expert_ids, slot_rank].astype(jnp.float32)
    moe_part = jnp.sum(picked * gate_weights[:, :, None], axis=1)
    moe_total = lax.psum(moe_part.astype(jnp.bfloat16), "dp").astype(jnp.float32)
    out = (residual + moe_total).astype(jnp.bfloat16)
    new_rows = got_kv.reshape(n_expert * kv_cap, kv_row.shape[1])
    return (out, new_rows)


def solution(mesh):
    placed = (
        P("expert", None),
        P(),
        P("expert", "dp"),
        P("expert", "dp"),
        P("expert", "dp"),
        P("expert", "dp"),
        P("expert", "dp"),
        P("expert", None),
        P("expert", None),
        P("expert", None),
        P("expert", None),
        P(),
        P("expert", None, "dp"),
        P("expert", None, "dp"),
        P("expert", "dp", None),
        P("expert", None),
        P("expert", None),
    )
    return jax.shard_map(
        local,
        mesh=mesh,
        in_specs=placed,
        out_specs=(P("expert", None), P("expert", "dp")),
        check_vma=False,
    )
```

profile of v0, /device:TPU:2, one launch (start us, length us, event | category | flops | bytes accessed | tf_op | source)
XLA Modules:
  0.0 761.0 jit_solution(5198881147081987779)
XLA Ops:
  11.7 6.5 copy.68
  18.2 4.0 fusion.85
  22.2 3.9 copy.82
  26.2 2.5 copy.83
  30.8 59.4 %all-gather.9.cloned.1.call-done = bf16[2048,512]{1,0:T(8,128)(2,1)} async-done(((bf16[32,512]{1,0:T(8,128)(2,1)}), bf16[2048,512]{1,0:T(8,128)(2,1)}) %all-gather.9.cloned.1.call-update) | async-done | bytes 2097168 | tf_op jit(solution)/shard_map/all_gather | solution.py:89
  92.9 75.0 %all-gather.5.cloned.1.call-done = bf16[2048,512]{1,0:T(8,128)(2,1)} async-done(((bf16[32,512]{1,0:T(8,128)(2,1)}), bf16[2048,512]{1,0:T(8,128)(2,1)}) %all-gather.5.cloned.1.call-update) | async-done | bytes 2097168 | tf_op jit(solution)/shard_map/all_gather | solution.py:90
  170.6 75.0 %all-gather.7.cloned.1.call-done = bf16[2048,512]{1,0:T(8,128)(2,1)} async-done(((bf16[32,512]{1,0:T(8,128)(2,1)}), bf16[2048,512]{1,0:T(8,128)(2,1)}) %all-gather.7.cloned.1.call-update) | async-done | bytes 2097168 | tf_op jit(solution)/shard_map/all_gather | solution.py:88
  245.6 2.7 fusion.37
  248.3 4.2 fusion.86
  252.6 2.8 fusion.34
  255.3 67.8 %all-gather.11.cloned.1.call-done = bf16[2048,512]{1,0:T(8,128)(2,1)} async-done(((bf16[32,512]{1,0:T(8,128)(2,1)}), bf16[2048,512]{1,0:T(8,128)(2,1)}) %all-gather.11.cloned.1.call-update) | async-done | bytes 2097168 | tf_op jit(solution)/shard_map/all_gather | solution.py:91
  323.2 3.1 convolution_convert_fusion
  326.8 3.8 gather_fusion.1
  330.9 41.1 %all-reduce.3.cloned.1.call-done = bf16[64,2048]{1,0:T(8,128)(2,1)} async-done(((bf16[64,2048]{1,0:T(8,128)(2,1)}), bf16[64,2048]{1,0:T(8,128)(2,1)}) %all-reduce.3.cloned.1.call-update) | async-done | bytes 262160 | tf_op jit(solution)/shard_map/psum | solution.py:125
  377.0 88.6 %scatter_fusion = bf16[64,16,2048]{2,1,0:T(8,128)(2,1)} fusion(bf16[64,16,2048]{2,1,0:T(8,128)(2,1)} %broadcast_in_dim.35, s32[512]{0:T(512)S(1)} %reshape.227, bf16[512,2048]{1,0:T(8,128)(2,1)S(1)} %broadcast_bitcast_fusion), kind=kCustom, calls=%fused_computation.3 | custom fusion | bytes 6295552 | tf_op jit(solution)/shard_map/scatter | solution.py:140
  465.7 107.1 %all_to_all.15 = bf16[64,1,16,2048]{3,2,1,0:T(8,128)(2,1)S(1)} all-to-all(bf16[64,1,16,2048]{3,2,1,0:T(8,128)(2,1)} %bitcast.152), channel_id=1, replica_groups=mesh['dp'=4,'expert'=64] {'expert'}, dimensions={0} | all-to-all | bytes 8388608 | tf_op jit(solution)/shard_map/all_to_all | solution.py:144
  576.0 8.5 %convert_bitcast_fusion = bf16[64,1,16,2048]{3,2,1,0:T(8,128)(2,1)} fusion(bf16[1,256,2048]{2,1,0:T(8,128)(2,1)S(1)} %copy-done, bf16[64,1,16,2048]{3,2,1,0:T(8,128)(2,1)} %copy-done.2, bf16[1,2048,256]{2,1,0:T(8,128)(2,1)S(1)} %copy-done.12, f32[64,1,16,256]{3,2,0,1:T(8,128)S(1)} %fusion.16), kind=kOutput, calls=%fused_computation.15 | convolution fusion | flops 2151153664 | bytes 11534336 | tf_op jit(solution)/shard_map/necf,efd->necd/dot_general | solution.py:55
  584.5 5.8 all-to-all-start.1
  592.3 9.3 %scatter_fusion.1 = bf16[64,2,1024]{2,1,0:T(2,128)(2,1)} fusion(bf16[64,2,1024]{2,1,0:T(2,128)(2,1)} %broadcast_in_dim.40, s32[64]{0:T(128)S(1)} %fusion.73, bf16[64,1024]{1,0:T(8,128)(2,1)S(1)} %pad_maximum_fusion), kind=kCustom, calls=%fused_computation.4 | custom fusion | bytes 393728 | tf_op jit(solution)/shard_map/scatter | solution.py:133
  601.6 84.8 %all-to-all-done.1 = bf16[64,1,16,2048]{3,2,1,0:T(8,128)(2,1)} async-done(((bf16[64,1,16,2048]{3,2,1,0:T(8,128)(2,1)}), bf16[64,1,16,2048]{3,2,1,0:T(8,128)(2,1)}, u32[]{:S(2)}, u32[]{:S(2)}) %all-to-all-start.1) | async-done | bytes 4194336 | tf_op jit(solution)/shard_map/all_to_all | solution.py:148
  686.4 5.6 all-to-all-start.2
  692.4 10.0 %gather_fusion = bf16[512,2048]{1,0:T(8,128)(2,1)S(1)} fusion(bf16[64,16,2048]{2,1,0:T(8,128)(2,1)} %bitcast.34, s32[512]{0:T(512)S(1)} %reshape.207), kind=kCustom, calls=%fused_computation | custom fusion | bytes 4198400 | tf_op jit(solution)/shard_map/gather | solution.py:151
  702.4 2.5 fusion.3
  706.7 45.6 %all-reduce.5.cloned.1.call-done = bf16[64,2048]{1,0:T(8,128)(2,1)} async-done(((bf16[64,2048]{1,0:T(8,128)(2,1)}), bf16[64,2048]{1,0:T(8,128)(2,1)}) %all-reduce.5.cloned.1.call-update) | async-done | bytes 262160 | tf_op jit(solution)/shard_map/psum | solution.py:153
  (89 shorter events, 26.8 us)
Async XLA Ops:
  7.2 568.9 %copy-start = (bf16[1,256,2048]{2,1,0:T(8,128)(2,1)S(1)}, bf16[1,256,2048]{2,1,0:T(8,128)(2,1)}, u32[]{:S(2)}) copy-start(bf16[1,256,2048]{2,1,0:T(8,128)(2,1)} %param.31) | copy-start | bytes 3145732
  7.2 83.0 %all-gather.9.cloned.1.call-start = ((), (), s32[]{:S(2)}) async-start(), calls=%async_computation.5 | async-start | bytes 2129920 | tf_op jit(solution)/shard_map/all_gather | solution.py:89
  7.9 160.0 %all-gather.5.cloned.1.call-start = ((), (), s32[]{:S(2)}) async-start(), calls=%async_computation.3 | async-start | bytes 2129920 | tf_op jit(solution)/shard_map/all_gather | solution.py:90
  8.7 237.0 %all-gather.7.cloned.1.call-start = ((), (), s32[]{:S(2)}) async-start(), calls=%async_computation.4 | async-start | bytes 2129920 | tf_op jit(solution)/shard_map/all_gather | solution.py:88
  9.4 313.8 %all-gather.11.cloned.1.call-start = ((), (), s32[]{:S(2)}) async-start(), calls=%async_computation.6 | async-start | bytes 2129920 | tf_op jit(solution)/shard_map/all_gather | solution.py:91
  10.0 362.0 %all-reduce.3.cloned.1.call-start = ((), (), s32[]{:S(2)}) async-start(), calls=%async_computation.7 | async-start | bytes 524288 | tf_op jit(solution)/shard_map/psum | solution.py:125
  26.2 2.5 copy-start.6
  26.2 3.3 copy-start.10
  26.2 3.4 copy-start.1
  26.2 63.9 %copy-start.5 = (f32[2048]{0:T(1024)S(1)}, f32[2048]{0:T(1024)}, u32[]{:S(2)}) copy-start(f32[2048]{0:T(1024)} %param.18) | copy-start | bytes 24580
  248.3 4.2 copy-start.3
  255.3 71.0 %copy-start.4 = (s32[64,8]{1,0:T(8,128)S(1)}, s32[64,8]{1,0:T(8,128)}, u32[]{:S(2)}) copy-start(s32[64,8]{1,0:T(8,128)} %copy.75) | copy-start | bytes 6148
  326.8 46.4 %copy-start.7 = (f32[2048]{0:T(1024)S(1)}, f32[2048]{0:T(1024)}, u32[]{:S(2)}) copy-start(f32[2048]{0:T(1024)} %param.28) | copy-start | bytes 24580
  465.7 109.1 %copy-start.11 = (bf16[1,2048,256]{2,1,0:T(8,128)(2,1)S(1)}, bf16[1,2048,256]{2,1,0:T(8,128)(2,1)}, u32[]{:S(2)}) copy-start(bf16[1,2048,256]{2,1,0:T(8,128)(2,1)} %param.29) | copy-start | bytes 3145732
  572.8 2.0 copy-start.2
  574.8 1.3 copy-start.12
  584.5 5.8 copy-start.9
  584.5 101.9 %all-to-all-start.1 = ((bf16[64,1,16,2048]{3,2,1,0:T(8,128)(2,1)}), bf16[64,1,16,2048]{3,2,1,0:T(8,128)(2,1)}, u32[]{:S(2)}, u32[]{:S(2)}) async-start(bf16[64,1,16,2048]{3,2,1,0:T(8,128)(2,1)} %convert_bitcast_fusion), calls=%async_computation.1 | async-start | bytes 8388608 | tf_op jit(solution)/shard_map/all_to_all | solution.py:148
  590.3 102.0 %copy-start.8 = (f32[64,8]{0,1:T(8,128)S(1)}, f32[64,8]{0,1:T(8,128)}, u32[]{:S(2)}) copy-start(f32[64,8]{0,1:T(8,128)} %param.33) | copy-start | bytes 6148
  686.4 18.5 %all-to-all-start.2 = ((bf16[64,2,1024]{2,1,0:T(2,128)(2,1)}), bf16[64,2,1024]{2,1,0:T(2,128)(2,1)}, u32[]{:S(2)}, u32[]{:S(2)}) async-start(bf16[64,2,1024]{2,1,0:T(2,128)(2,1)} %scatter_fusion.1), calls=%async_computation.2 | async-start | bytes 524288 | tf_op jit(solution)/shard_map/all_to_all | solution.py:145
  692.1 60.3 %all-reduce.5.cloned.1.call-start = ((), (), s32[]{:S(2)}) async-start(), calls=%async_computation.8 | async-start | bytes 524288 | tf_op jit(solution)/shard_map/psum | solution.py:153
Sparse Core Ops, SparseCore 0:
  10.8 79.3 all-gather.8
  92.9 74.9 all-gather.4
  170.6 74.9 all-gather.6
  248.2 74.9 all-gather.10
  326.4 45.5 all-reduce.2
  705.1 47.2 all-reduce.4
where the time goes:
time: 765 us; the launch traced here: 761 us
  waiting for transfers between devices  451 us (59%)
  local copies, waits for them, and re-layouts  140 us (18%)
  blocking collectives  107 us (14%)
  matrix products  26.8 us (4%)
  between operations  14.4 us (2%)
  starting transfers between devices  11.6 us (2%)
  other arithmetic  10.1 us (1%)
    all_to_all x1, blocking collectives, local(): lax.all_to_all(tok_buffer, 'expert', split_axis=0, concat_axis=0, tiled=T...  107 us
    scatter x1, local copies, waits for them, and re-layouts, local(): tok_buffer = jnp.zeros((experts_all, capacity, model_width), jnp.bfloat16...  88.6 us
    all_to_all x1, waiting for transfers between devices, local(): lax.all_to_all(partial_value, 'expert', split_axis=0, concat_axis=0, tile...  84.8 us
    all_gather x1, waiting for transfers between devices, local(): lax.all_gather(w_value, 'expert', axis=0, tiled=True)  75 us
    all_gather x1, waiting for transfers between devices, local(): lax.all_gather(w_query, 'expert', axis=0, tiled=True)  75 us
    all_gather x1, waiting for transfers between devices, local(): lax.all_gather(w_out, 'expert', axis=0, tiled=True)  67.8 us
    all_gather x1, waiting for transfers between devices, local(): lax.all_gather(w_key, 'expert', axis=0, tiled=True)  59.4 us
    psum x1, waiting for transfers between devices, local(): lax.psum(moe_part.astype(jnp.bfloat16), 'dp').astype(jnp.float32)  45.6 us
  transfers between devices with their start and end apart: 8, of which 7 were waited for; matrix products, arithmetic and copies ran while one was open for 9% of the time, Pallas kernels for 0%

commit v1 on v0

--- a/solution.py
+++ b/solution.py
@@ -88,7 +88,9 @@
         lax.all_gather(w_query, "expert", axis=0, tiled=True),
         lax.all_gather(w_key, "expert", axis=0, tiled=True),
         lax.all_gather(w_value, "expert", axis=0, tiled=True),
-        lax.all_gather(w_out, "expert", axis=0, tiled=True),
+        jnp.concatenate(
+            lax.all_to_all(jnp.stack([w_out] * lax.axis_size("expert")), "expert", 0, 0), axis=0
+        ),
     )
     resid_in = tokens.astype(jnp.float32)
     normed = norm_rows(resid_in, attn_gain)

time: 765 us -> 698 us (0.912)
  waiting for transfers between devices: 451 us -> 369 us
  starting transfers between devices: 11.6 us -> 23.6 us
    all_gather x1 -> x0, waiting for transfers between devices: 67.8 us -> none  [local(): lax.all_gather(w_out, 'expert', axis=0, tiled=True)]
    all_gather x1, waiting for transfers between devices: 59.4 us -> 45.8 us  [local(): lax.all_gather(w_key, 'expert', axis=0, tiled=True)]
    all_to_all x0 -> x1, starting transfers between devices: none -> 12 us  [local(): lax.all_to_all(jnp.stack([w_out] * lax.axis_size('expert')), 'expert', 0, 0)]
    unnamed x32 -> x38, local copies, waits for them, and re-layouts: 15.7 us -> 17.3 us
  transfers between devices with their start and end apart: 8 -> 8, of which waited for: 7 -> 6; matrix products, arithmetic and copies ran while one was open for 9% -> 10% of each run, Pallas kernels for 0% -> 0%
where the time goes in v1:
time: 698 us; the launch traced here: 694 us
  waiting for transfers between devices  369 us (53%)
  local copies, waits for them, and re-layouts  144 us (21%)
  blocking collectives  107 us (15%)
  matrix products  26.6 us (4%)
  starting transfers between devices  23.6 us (3%)
  between operations  14.1 us (2%)
  other arithmetic  10.1 us (1%)
    all_to_all x1, blocking collectives, local(): lax.all_to_all(tok_buffer, 'expert', split_axis=0, concat_axis=0, tiled=T...  107 us
    scatter x1, local copies, waits for them, and re-layouts, local(): tok_buffer = jnp.zeros((experts_all, capacity, model_width), jnp.bfloat16...  88.4 us
    all_to_all x1, waiting for transfers between devices, local(): lax.all_to_all(partial_value, 'expert', split_axis=0, concat_axis=0, tile...  84.8 us
    all_gather x1, waiting for transfers between devices, local(): lax.all_gather(w_query, 'expert', axis=0, tiled=True)  75 us
    all_gather x1, waiting for transfers between devices, local(): lax.all_gather(w_value, 'expert', axis=0, tiled=True)  74.8 us
    all_gather x1, waiting for transfers between devices, local(): lax.all_gather(w_key, 'expert', axis=0, tiled=True)  45.8 us
    psum x1, waiting for transfers between devices, local(): lax.psum(moe_part.astype(jnp.bfloat16), 'dp').astype(jnp.float32)  45.6 us
    psum x1, waiting for transfers between devices, local(): lax.psum(attn_part.astype(jnp.bfloat16), 'dp').astype(jnp.float32)  40.3 us
  transfers between devices with their start and end apart: 8, of which 6 were waited for; matrix products, arithmetic and copies ran while one was open for 10% of the time, Pallas kernels for 0%

profile of v1, /device:TPU:2, one launch (start us, length us, event | category | flops | bytes accessed | tf_op | source)
XLA Modules:
  0.0 693.7 jit_solution(10901048764434220084)
XLA Ops:
  11.0 12.0 %all-to-all-start = ((bf16[64,32,512]{2,1,0:T(8,128)(2,1)}), bf16[64,32,512]{2,1,0:T(8,128)(2,1)S(1)}, u32[]{:S(2)}, u32[]{:S(2)}) async-start(bf16[64,32,512]{2,1,0:T(8,128)(2,1)} %stack.2), calls=%async_computation | async-start | bytes 4194304 | tf_op jit(solution)/shard_map/all_to_all | solution.py:92
  23.8 6.5 copy.68
  30.3 4.9 fusion.85
  35.2 4.0 copy.82
  39.2 4.0 copy.83
  46.2 45.8 %all-gather.8.cloned.1.call-done = bf16[2048,512]{1,0:T(8,128)(2,1)} async-done(((bf16[32,512]{1,0:T(8,128)(2,1)}), bf16[2048,512]{1,0:T(8,128)(2,1)}) %all-gather.8.cloned.1.call-update) | async-done | bytes 2097168 | tf_op jit(solution)/shard_map/all_gather | solution.py:89
  94.8 74.8 %all-gather.4.cloned.1.call-done = bf16[2048,512]{1,0:T(8,128)(2,1)} async-done(((bf16[32,512]{1,0:T(8,128)(2,1)}), bf16[2048,512]{1,0:T(8,128)(2,1)}) %all-gather.4.cloned.1.call-update) | async-done | bytes 2097168 | tf_op jit(solution)/shard_map/all_gather | solution.py:90
  172.4 75.0 %all-gather.6.cloned.1.call-done = bf16[2048,512]{1,0:T(8,128)(2,1)} async-done(((bf16[32,512]{1,0:T(8,128)(2,1)}), bf16[2048,512]{1,0:T(8,128)(2,1)}) %all-gather.6.cloned.1.call-update) | async-done | bytes 2097168 | tf_op jit(solution)/shard_map/all_gather | solution.py:88
  247.3 2.7 fusion.37
  250.1 4.1 fusion.86
  254.2 3.4 fusion.34
  261.2 3.8 gather_fusion.1
  265.3 40.3 %all-reduce.3.cloned.1.call-done = bf16[64,2048]{1,0:T(8,128)(2,1)} async-done(((bf16[64,2048]{1,0:T(8,128)(2,1)}), bf16[64,2048]{1,0:T(8,128)(2,1)}) %all-reduce.3.cloned.1.call-update) | async-done | bytes 262160 | tf_op jit(solution)/shard_map/psum | solution.py:127
  308.2 2.5 broadcast_in_dim.35
  310.6 88.4 %scatter_fusion = bf16[64,16,2048]{2,1,0:T(8,128)(2,1)} fusion(bf16[64,16,2048]{2,1,0:T(8,128)(2,1)} %broadcast_in_dim.35, s32[512]{0:T(512)S(1)} %reshape.233, bf16[512,2048]{1,0:T(8,128)(2,1)S(1)} %broadcast_bitcast_fusion), kind=kCustom, calls=%fused_computation.3 | custom fusion | bytes 6295552 | tf_op jit(solution)/shard_map/scatter | solution.py:142
  399.0 106.9 %all_to_all.20 = bf16[64,1,16,2048]{3,2,1,0:T(8,128)(2,1)S(1)} all-to-all(bf16[64,1,16,2048]{3,2,1,0:T(8,128)(2,1)} %bitcast.153), channel_id=1, replica_groups=mesh['dp'=4,'expert'=64] {'expert'}, dimensions={0} | all-to-all | bytes 8388608 | tf_op jit(solution)/shard_map/all_to_all | solution.py:146
  509.1 8.5 %convert_bitcast_fusion = bf16[64,1,16,2048]{3,2,1,0:T(8,128)(2,1)} fusion(bf16[1,256,2048]{2,1,0:T(8,128)(2,1)S(1)} %copy-done, bf16[64,1,16,2048]{3,2,1,0:T(8,128)(2,1)} %copy-done.2, bf16[1,2048,256]{2,1,0:T(8,128)(2,1)S(1)} %copy-done.13, f32[64,1,16,256]{3,2,0,1:T(8,128)S(1)} %fusion.16), kind=kOutput, calls=%fused_computation.15 | convolution fusion | flops 2151153664 | bytes 11534336 | tf_op jit(solution)/shard_map/necf,efd->necd/dot_general | solution.py:55
  517.6 5.7 all-to-all-start.2
  525.3 9.3 %scatter_fusion.1 = bf16[64,2,1024]{2,1,0:T(2,128)(2,1)} fusion(bf16[64,2,1024]{2,1,0:T(2,128)(2,1)} %broadcast_in_dim.40, s32[64]{0:T(128)S(1)} %fusion.73, bf16[64,1024]{1,0:T(8,128)(2,1)S(1)} %pad_maximum_fusion), kind=kCustom, calls=%fused_computation.4 | custom fusion | bytes 393728 | tf_op jit(solution)/shard_map/scatter | solution.py:135
  534.7 84.8 %all-to-all-done.2 = bf16[64,1,16,2048]{3,2,1,0:T(8,128)(2,1)} async-done(((bf16[64,1,16,2048]{3,2,1,0:T(8,128)(2,1)}), bf16[64,1,16,2048]{3,2,1,0:T(8,128)(2,1)}, u32[]{:S(2)}, u32[]{:S(2)}) %all-to-all-start.2) | async-done | bytes 4194336 | tf_op jit(solution)/shard_map/all_to_all | solution.py:150
  619.5 5.6 all-to-all-start.3
  625.4 10.0 %gather_fusion = bf16[512,2048]{1,0:T(8,128)(2,1)S(1)} fusion(bf16[64,16,2048]{2,1,0:T(8,128)(2,1)} %bitcast.35, s32[512]{0:T(512)S(1)} %reshape.213), kind=kCustom, calls=%fused_computation | custom fusion | bytes 4198400 | tf_op jit(solution)/shard_map/gather | solution.py:153
  635.4 2.5 fusion.3
  639.8 45.6 %all-reduce.5.cloned.1.call-done = bf16[64,2048]{1,0:T(8,128)(2,1)} async-done(((bf16[64,2048]{1,0:T(8,128)(2,1)}), bf16[64,2048]{1,0:T(8,128)(2,1)}) %all-reduce.5.cloned.1.call-update) | async-done | bytes 262160 | tf_op jit(solution)/shard_map/psum | solution.py:155
  (95 shorter events, 28.5 us)
Async XLA Ops:
  7.2 501.9 %copy-start = (bf16[1,256,2048]{2,1,0:T(8,128)(2,1)S(1)}, bf16[1,256,2048]{2,1,0:T(8,128)(2,1)}, u32[]{:S(2)}) copy-start(bf16[1,256,2048]{2,1,0:T(8,128)(2,1)} %param.31) | copy-start | bytes 3145732
  7.2 84.8 %all-gather.8.cloned.1.call-start = ((), (), s32[]{:S(2)}) async-start(), calls=%async_computation.6 | async-start | bytes 2129920 | tf_op jit(solution)/shard_map/all_gather | solution.py:89
  7.9 161.7 %all-gather.4.cloned.1.call-start = ((), (), s32[]{:S(2)}) async-start(), calls=%async_computation.4 | async-start | bytes 2129920 | tf_op jit(solution)/shard_map/all_gather | solution.py:90
  11.0 246.6 %all-to-all-start = ((bf16[64,32,512]{2,1,0:T(8,128)(2,1)}), bf16[64,32,512]{2,1,0:T(8,128)(2,1)S(1)}, u32[]{:S(2)}, u32[]{:S(2)}) async-start(bf16[64,32,512]{2,1,0:T(8,128)(2,1)} %stack.2), calls=%async_computation | async-start | bytes 4194304 | tf_op jit(solution)/shard_map/all_to_all | solution.py:92
  23.0 224.3 %all-gather.6.cloned.1.call-start = ((), (), s32[]{:S(2)}) async-start(), calls=%async_computation.5 | async-start | bytes 2129920 | tf_op jit(solution)/shard_map/all_gather | solution.py:88
  23.8 281.9 %all-reduce.3.cloned.1.call-start = ((), (), s32[]{:S(2)}) async-start(), calls=%async_computation.7 | async-start | bytes 524288 | tf_op jit(solution)/shard_map/psum | solution.py:127
  39.1 4.1 copy-start.4
  39.1 4.8 copy-start.14
  39.1 4.9 copy-start.15
  39.2 5.2 copy-start.11
  39.2 5.3 copy-start.1
  39.2 52.9 %copy-start.3 = (f32[2048]{0:T(1024)S(1)}, f32[2048]{0:T(1024)}, u32[]{:S(2)}) copy-start(f32[2048]{0:T(1024)} %param.18) | copy-start | bytes 24580
  44.6 50.2 %copy-start.7 = (f32[64]{0:T(128)}, f32[64]{0:T(128)S(1)}, u32[]{:S(2)}) copy-start(f32[64]{0:T(128)S(1)} %add_rsqrt_fusion.1) | copy-start | bytes 772
  169.6 77.7 %copy-start.8 = (f32[64]{0:T(128)S(1)}, f32[64]{0:T(128)}, u32[]{:S(2)}) copy-start(f32[64]{0:T(128)} %copy-done.7) | copy-start | bytes 772
  257.6 3.4 copy-start.5
  261.2 45.6 %copy-start.6 = (f32[2048]{0:T(1024)S(1)}, f32[2048]{0:T(1024)}, u32[]{:S(2)}) copy-start(f32[2048]{0:T(1024)} %param.28) | copy-start | bytes 24580
  399.0 108.8 %copy-start.12 = (bf16[1,2048,256]{2,1,0:T(8,128)(2,1)S(1)}, bf16[1,2048,256]{2,1,0:T(8,128)(2,1)}, u32[]{:S(2)}) copy-start(bf16[1,2048,256]{2,1,0:T(8,128)(2,1)} %param.29) | copy-start | bytes 3145732
  505.9 1.9 copy-start.2
  507.8 1.3 copy-start.13
  517.6 5.8 copy-start.10
  517.6 101.9 %all-to-all-start.2 = ((bf16[64,1,16,2048]{3,2,1,0:T(8,128)(2,1)}), bf16[64,1,16,2048]{3,2,1,0:T(8,128)(2,1)}, u32[]{:S(2)}, u32[]{:S(2)}) async-start(bf16[64,1,16,2048]{3,2,1,0:T(8,128)(2,1)} %convert_bitcast_fusion), calls=%async_computation.2 | async-start | bytes 8388608 | tf_op jit(solution)/shard_map/all_to_all | solution.py:150
  523.3 102.0 %copy-start.9 = (f32[64,8]{0,1:T(8,128)S(1)}, f32[64,8]{0,1:T(8,128)}, u32[]{:S(2)}) copy-start(f32[64,8]{0,1:T(8,128)} %param.33) | copy-start | bytes 6148
  619.5 18.5 %all-to-all-start.3 = ((bf16[64,2,1024]{2,1,0:T(2,128)(2,1)}), bf16[64,2,1024]{2,1,0:T(2,128)(2,1)}, u32[]{:S(2)}, u32[]{:S(2)}) async-start(bf16[64,2,1024]{2,1,0:T(2,128)(2,1)} %scatter_fusion.1), calls=%async_computation.3 | async-start | bytes 524288 | tf_op jit(solution)/shard_map/all_to_all | solution.py:147
  625.1 60.3 %all-reduce.5.cloned.1.call-start = ((), (), s32[]{:S(2)}) async-start(), calls=%async_computation.8 | async-start | bytes 524288 | tf_op jit(solution)/shard_map/psum | solution.py:155
Sparse Core Ops, SparseCore 0:
  10.8 81.2 all-gather.7
  94.8 74.7 all-gather.3
  172.4 74.9 all-gather.5
  260.1 45.5 all-reduce.2
  638.1 47.2 all-reduce.4
